TPU v7x, 256 devices: a whole 4x4x8 slice. The times are simulated.
256 devices in a mesh: nodes: 64 (over z, y, core), mp: 4 (over x).
Axes of the slice: x: 4, y: 4, z: 8, core: 2. Of those that a mesh axis runs over, the one named last changes fastest.
Arguments:
- event_feats: bfloat16 [65536, 512], P('nodes'), may hold values from -6 to 6
- event_owner: int32 [65536, 1], P('nodes'), may hold values from 0 to 63; in each aligned block of 1024 rows (0 to 1023, 1024 to 2047, ...) at most 32 rows name the same one
- event_slot: int32 [65536], P('nodes'), may hold values from 0 to 255
- memory: bfloat16 [16384, 1024], P('nodes'), may hold values from -6 to 6
- w_msg_event: bfloat16 [512, 2048], P(None, 'mp'), may hold values from -0.25 to 0.25
- w_msg_state: bfloat16 [1024, 2048], P(None, 'mp'), may hold values from -0.1875 to 0.1875
- b_msg: float32 [2048], P('mp'), may hold values from -3 to 3
- w_msg_out: bfloat16 [2048, 1024], P('mp'), may hold values from -0.125 to 0.125
- b_out: float32 [1024], replicated, may hold values from -3 to 3
- w_input: bfloat16 [3, 1024, 1024], P(None, None, 'mp'), may hold values from -0.1875 to 0.1875
- w_hidden: bfloat16 [3, 1024, 1024], P(None, None, 'mp'), may hold values from -0.1875 to 0.1875
- b_input: float32 [3, 1024], P(None, 'mp'), may hold values from -3 to 3
- b_hidden: float32 [3, 1024], P(None, 'mp'), may hold values from -3 to 3
- state_slots: int32 [4096, 32], P('nodes'), may hold values from 0 to 255
- neighbours: int32 [16384, 10], P('nodes'), may hold values from 0 to 2047
- query_slots: int32 [16384], P('nodes'), may hold values from 0 to 255
- w_neigh: bfloat16 [1024, 1024], P('mp'), may hold values from -0.1875 to 0.1875
- w_self: bfloat16 [1024, 1024], P('mp'), may hold values from -0.1875 to 0.1875
- b_embed: float32 [1024], replicated, may hold values from -3 to 3
Outputs:
- new_memory: bfloat16 [16384, 1024], P('nodes', 'mp')
- embedding: bfloat16 [16384, 1024], P(('nodes', 'mp'))
Inputs may be any that keep to these rules, and one draw needn't show every extreme that they name: `event_owner`: among the 1024 events of one block of events, at most 32 name the same owner, and in every draw some owner is named exactly 32 times by some block.
All inputs are finite; a program needn't handle non-finite values.
Results may differ from a plain program's by a relative error of at most 0.014.
Values may be sent and summed in bfloat16 or wider, within the bound.
No kernel may reach another device: no remote copies, remote signals or barrier semaphores. Data moves between devices by JAX's collectives and lax.ppermute only.
A program may use at most 64 MiB of HBM per device.

v0:
```python
import jax
import jax.numpy as jnp
from jax import lax
from jax.sharding import PartitionSpec as P


def per_device(
    event_feats,
    event_owner,
    event_slot,
    memory,
    w_msg_event,
    w_msg_state,
    b_msg,
    w_msg_out,
    b_out,
    w_input,
    w_hidden,
    b_input,
    b_hidden,
    state_slots,
    neighbours,
    query_slots,
    w_neigh,
    w_self,
    b_embed,
):
    owner_count = lax.axis_size("nodes")
    share_count = lax.axis_size("mp")
    mp_index = lax.axis_index("mp")
    event_rows = event_feats.shape[0]
    feat_width = event_feats.shape[1]
    mem_rows = memory.shape[0]
    mem_width = memory.shape[1]
    col_share = mem_width // share_count
    capacity = 2 * event_rows // owner_count
    owner = event_owner[:, 0]
    match = (owner[:, None] == lax.broadcasted_iota(jnp.int32, (1, owner_count), 1)).astype(
        jnp.int32
    )
    before = jnp.cumsum(match, axis=0) - match
    place = jnp.sum(before * match, axis=1)
    target = owner * capacity + place
    id_buffer = jnp.full((owner_count * capacity,), -1, jnp.int32).at[target].set(event_slot)
    id_buffer = id_buffer.reshape(owner_count, capacity)
    feat_buffer = (
        jnp.zeros((owner_count * capacity, feat_width), jnp.bfloat16).at[target].set(event_feats)
    )
    feat_buffer = feat_buffer.reshape(owner_count, capacity, feat_width)
    arrived = lax.all_to_all(feat_buffer, "nodes", split_axis=0, concat_axis=0, tiled=True)
    arrived_ids = lax.all_to_all(id_buffer, "nodes", split_axis=0, concat_axis=0, tiled=True)
    recv_rows = owner_count * capacity
    arrived = arrived.reshape(recv_rows, feat_width)
    arrived_ids = arrived_ids.reshape(recv_rows)
    valid = arrived_ids >= 0
    safe_ids = jnp.where(valid, arrived_ids, 0)
    segment_ids = jnp.where(valid, arrived_ids, mem_rows)
    state_proj = jnp.dot(memory, w_msg_state, preferred_element_type=jnp.float32)
    pre = (
        jnp.dot(arrived, w_msg_event, preferred_element_type=jnp.float32)
        + jnp.take(state_proj, safe_ids, axis=0)
        + b_msg
    )
    hidden_msg = jax.nn.relu(pre).astype(jnp.bfloat16)
    partial_msg = jnp.dot(hidden_msg, w_msg_out, preferred_element_type=jnp.float32)
    partial_total = jax.ops.segment_sum(partial_msg, segment_ids, num_segments=mem_rows + 1)[
        :mem_rows
    ]
    counts = jax.ops.segment_sum(valid.astype(jnp.float32), segment_ids, num_segments=mem_rows + 1)[
        :mem_rows
    ]
    divisor = jnp.maximum(counts, 1.0)[:, None]
    msg_total = lax.psum(partial_total.astype(jnp.bfloat16), "mp").astype(jnp.float32)
    aggregate = (msg_total / divisor + b_out).astype(jnp.bfloat16)
    gates_in = (
        jnp.einsum("nd,gdc->gnc", aggregate, w_input, preferred_element_type=jnp.float32)
        + b_input[:, None, :]
    )
    gates_st = (
        jnp.einsum("nd,gdc->gnc", memory, w_hidden, preferred_element_type=jnp.float32)
        + b_hidden[:, None, :]
    )
    reset_gate = jax.nn.sigmoid(gates_in[0] + gates_st[0])
    update_gate = jax.nn.sigmoid(gates_in[1] + gates_st[1])
    candidate = jnp.tanh(gates_in[2] + reset_gate * gates_st[2])
    old_state = lax.dynamic_slice_in_dim(memory, mp_index * col_share, col_share, 1).astype(
        jnp.float32
    )
    updated = (1.0 - update_gate) * candidate + update_gate * old_state
    new_memory = jnp.where((counts > 0.0)[:, None], updated, old_state).astype(jnp.bfloat16)
    outgoing = jnp.take(new_memory, state_slots, axis=0)
    relayed = lax.all_to_all(outgoing, "nodes", split_axis=0, concat_axis=0, tiled=True)
    relayed = relayed.reshape(relayed.shape[0] * relayed.shape[1], col_share)
    neigh_rows = jnp.take(relayed, neighbours, axis=0).astype(jnp.float32)
    neigh_mean = (jnp.sum(neigh_rows, axis=1) / neighbours.shape[1]).astype(jnp.bfloat16)
    self_state = jnp.take(new_memory, query_slots, axis=0)
    summed = lax.psum_scatter(
        (
            jnp.dot(neigh_mean, w_neigh, preferred_element_type=jnp.float32)
            + jnp.dot(self_state, w_self, preferred_element_type=jnp.float32)
        ).astype(jnp.bfloat16),
        "mp",
        scatter_dimension=0,
        tiled=True,
    ).astype(jnp.float32)
    embedding = jax.nn.relu(summed + b_embed).astype(jnp.bfloat16)
    return (new_memory, embedding)


def solution(mesh):
    in_specs = (
        P("nodes", None),
        P("nodes", None),
        P("nodes"),
        P("nodes", None),
        P(None, "mp"),
        P(None, "mp"),
        P("mp"),
        P("mp", None),
        P(),
        P(None, None, "mp"),
        P(None, None, "mp"),
        P(None, "mp"),
        P(None, "mp"),
        P("nodes", None),
        P("nodes", None),
        P("nodes"),
        P("mp", None),
        P("mp", None),
        P(),
    )
    out_specs = (P("nodes", "mp"), P(("nodes", "mp"), None))
    return jax.shard_map(
        per_device, mesh=mesh, in_specs=in_specs, out_specs=out_specs, check_vma=False
    )
```

profile of v0, /device:TPU:8, one launch (start us, length us, event | category | flops | bytes accessed | tf_op | source)
XLA Modules:
  0.0 281.5 jit_solution(5040244256541828532)
XLA Ops:
  8.0 18.0 %reduce-window.6 = s32[64,8,128]{2,1,0:T(8,128)S(1)} reduce-window(s32[64,8,128]{2,1,0:T(8,128)S(1)} %fusion.31, s32[]{:T(128)} %constant.48.clone.1), window={size=1x1x128 pad=0_0x0_0x127_0}, to_apply=%region_0.0 | reduce-window | flops 8323072 | bytes 524292 | tf_op jit(solution)/shard_map/reduce-window
  26.7 4.5 %scatter_custom_fusion = s32[2048]{0:T(1024)S(1)} fusion(s32[1024]{0:T(1024)S(1)} %bitcast.71, s32[1024]{0:T(1024)} %param.21, s32[]{:T(128)} %constant.46.clone.1), kind=kCustom, calls=%fused_computation.79 | custom fusion | bytes 8704 | tf_op jit(solution)/shard_map/scatter | solution.py:44
  31.9 12.1 %all-to-all-start = ((s32[64,1,32]{2,1,0:T(1,128)}), s32[64,1,32]{2,1,0:T(1,128)S(1)}, u32[]{:S(2)}, u32[]{:S(2)}) async-start(s32[64,1,32]{2,1,0:T(1,128)} %bitcast.6), calls=%async_computation | async-start | bytes 65536 | tf_op jit(solution)/shard_map/all_to_all | solution.py:51
  44.0 7.2 %scatter_custom_fusion.2 = bf16[2048,512]{1,0:T(8,128)(2,1)} fusion(s32[1024]{0:T(1024)S(1)} %bitcast.72, bf16[1024,512]{1,0:T(8,128)(2,1)} %param.19, bf16[]{:T(256)} %constant.58.clone.1), kind=kCustom, calls=%fused_computation.18 | custom fusion | bytes 2097664 | tf_op jit(solution)/shard_map/scatter | solution.py:47
  51.2 1.4 all-to-all-done
  52.5 9.3 %all-to-all-start.1 = ((bf16[64,32,512]{2,1,0:T(8,128)(2,1)}), bf16[64,32,512]{2,1,0:T(8,128)(2,1)}, u32[]{:S(2)}, u32[]{:S(2)}) async-start(bf16[64,32,512]{2,1,0:T(8,128)(2,1)} %bitcast.60), calls=%async_computation.1 | async-start | bytes 4194304 | tf_op jit(solution)/shard_map/all_to_all | solution.py:50
  62.2 1.5 fusion.45
  63.7 1.6 fusion.1
  66.8 9.0 %gather_fusion = f32[2048,512]{1,0:T(8,128)} fusion(f32[256,512]{1,0:T(8,128)S(1)} %fusion.45, s32[2048]{0:T(1024)S(1)} %broadcast_clamp_fusion.1), kind=kCustom, calls=%fused_computation | custom fusion | bytes 8396800 | tf_op jit(solution)/shard_map/jit(_take)/gather | solution.py:61
  75.8 37.1 %all-to-all-done.1 = bf16[64,32,512]{2,1,0:T(8,128)(2,1)} async-done(((bf16[64,32,512]{2,1,0:T(8,128)(2,1)}), bf16[64,32,512]{2,1,0:T(8,128)(2,1)}, u32[]{:S(2)}, u32[]{:S(2)}) %all-to-all-start.1) | async-done | bytes 2097184 | tf_op jit(solution)/shard_map/all_to_all | solution.py:50
  113.0 7.9 %fusion.5 = f32[2048,1024]{1,0:T(8,128)} fusion(bf16[512,1024]{1,0:T(8,128)(2,1)} %param.26, f32[2048,512]{1,0:T(8,128)} %gather_fusion, bf16[2048,512]{1,0:T(8,128)(2,1)} %bitcast.9, bf16[512,512]{1,0:T(8,128)(2,1)S(1)} %copy-done.10, f32[512]{0:T(512)S(1)} %copy-done.14, pred[2048]{0:T(1024)(128)(4,1)S(1)} %get-tuple-element.3), kind=kOutput, calls=%fused_computation.21 | convolution fusion | flops 3226468352 | bytes 16257024 | tf_op jit(solution)/shard_map/dot_general | solution.py:65
  120.8 19.2 %scatter_custom_fusion.3 = f32[257,1024]{1,0:T(8,128)S(1)} fusion(s32[2048]{0:T(1024)S(1)} %bitcast.69, f32[2048,1024]{1,0:T(8,128)} %fusion.5, f32[]{:T(128)} %constant.39.clone.1), kind=kCustom, calls=%fused_computation.22 | custom fusion | flops 2097152 | bytes 1053184 | tf_op jit(solution)/shard_map/scatter-add | solution.py:66
  141.1 14.7 %scatter_custom_fusion.1 = f32[257]{0:T(512)S(1)} fusion(s32[2048]{0:T(1024)S(1)} %bitcast.70, f32[2048]{0:T(1024)S(1)} %get-tuple-element.2, f32[]{:T(128)} %constant.39.clone.1), kind=kCustom, calls=%fused_computation.83 | custom fusion | flops 2048 | bytes 1032 | tf_op jit(solution)/shard_map/scatter-add | solution.py:69
  155.8 29.8 %all-reduce.2.cloned.1.call-done = bf16[256,1024]{1,0:T(8,128)(2,1)} async-done(((bf16[256,1024]{1,0:T(8,128)(2,1)}), bf16[256,1024]{1,0:T(8,128)(2,1)}) %all-reduce.2.cloned.1.call-update) | async-done | bytes 524304 | tf_op jit(solution)/shard_map/psum | solution.py:73
  185.6 2.2 fusion.2
  188.9 7.5 %gather_fusion.1 = bf16[2048,256]{1,0:T(8,128)(2,1)S(1)} fusion(bf16[256,256]{1,0:T(8,128)(2,1)S(1)} %fusion.14, s32[2048]{0:T(1024)S(1)} %broadcast_clamp_fusion), kind=kCustom, calls=%fused_computation.1 | custom fusion | bytes 2105344 | tf_op jit(solution)/shard_map/jit(_take)/gather | solution.py:91
  196.4 1.3 broadcast_select_fusion
  197.7 10.6 %all-to-all-start.2 = ((bf16[64,32,256]{2,1,0:T(8,128)(2,1)}), bf16[64,32,256]{2,1,0:T(8,128)(2,1)S(1)}, u32[]{:S(2)}, u32[]{:S(2)}) async-start(bf16[64,32,256]{2,1,0:T(8,128)(2,1)} %broadcast_select_fusion), calls=%async_computation.2 | async-start | bytes 2097152 | tf_op jit(solution)/shard_map/all_to_all | solution.py:92
  210.2 26.8 %all-to-all-done.2 = bf16[64,32,256]{2,1,0:T(8,128)(2,1)S(1)} async-done(((bf16[64,32,256]{2,1,0:T(8,128)(2,1)}), bf16[64,32,256]{2,1,0:T(8,128)(2,1)S(1)}, u32[]{:S(2)}, u32[]{:S(2)}) %all-to-all-start.2) | async-done | bytes 1048608 | tf_op jit(solution)/shard_map/all_to_all | solution.py:92
  237.0 8.1 %gather_fusion.2 = bf16[2560,256]{1,0:T(8,128)(2,1)} fusion(bf16[2048,256]{1,0:T(8,128)(2,1)S(1)} %bitcast.59, s32[3072]{0:T(1024)S(1)} %pad_clamp_fusion), kind=kCustom, calls=%fused_computation.2 | custom fusion | bytes 2631680 | tf_op jit(solution)/shard_map/jit(_take)/gather | solution.py:94
  245.2 3.6 %reshape.152 = bf16[256,10,256]{2,1,0:T(8,128)(2,1)} reshape(bf16[2560,256]{1,0:T(8,128)(2,1)} %gather_fusion.2) | data formatting | bytes 2621440 | tf_op jit(solution)/shard_map/jit(_take)/gather | solution.py:94
  248.8 2.7 convert_reduce_fusion
  253.1 20.0 %reduce-scatter.2.cloned.1.call-done = bf16[64,1024]{1,0:T(8,128)(2,1)} async-done(((bf16[256,1024]{1,0:T(8,128)(2,1)}), bf16[64,1024]{1,0:T(8,128)(2,1)}) %reduce-scatter.2.cloned.1.call-update) | async-done | bytes 131088 | tf_op jit(solution)/shard_map/reduce_scatter | solution.py:97
  273.0 1.6 maximum_convert_fusion.1
  (73 shorter events, 9.5 us)
Async XLA Ops:
  7.2 56.6 %copy-start = (bf16[3,1024,256]{2,1,0:T(8,128)(2,1)S(1)}, bf16[3,1024,256]{2,1,0:T(8,128)(2,1)}, u32[]{:S(2)}) copy-start(bf16[3,1024,256]{2,1,0:T(8,128)(2,1)} %param.29) | copy-start | bytes 4718596
  7.2 19.4 %copy-start.7 = (s32[1024,1]{0,1:T(1,128)S(1)}, s32[1024,1]{0,1:T(1,128)}, u32[]{:S(2)}) copy-start(s32[1024,1]{0,1:T(1,128)} %param.20) | copy-start | bytes 12292
  31.9 20.7 %all-to-all-start = ((s32[64,1,32]{2,1,0:T(1,128)}), s32[64,1,32]{2,1,0:T(1,128)S(1)}, u32[]{:S(2)}, u32[]{:S(2)}) async-start(s32[64,1,32]{2,1,0:T(1,128)} %bitcast.6), calls=%async_computation | async-start | bytes 65536 | tf_op jit(solution)/shard_map/all_to_all | solution.py:51
  52.5 9.5 %copy-start.5 = (s32[64,32]{0,1:T(8,128)S(1)}, s32[64,32]{0,1:T(8,128)}, u32[]{:S(2)}) copy-start(s32[64,32]{0,1:T(8,128)} %param.32) | copy-start | bytes 24580
  52.5 9.7 %copy-start.2 = (bf16[1024,512]{1,0:T(8,128)(2,1)S(1)}, bf16[1024,512]{1,0:T(8,128)(2,1)}, u32[]{:S(2)}) copy-start(bf16[1024,512]{1,0:T(8,128)(2,1)} %param.24) | copy-start | bytes 3145732
  52.5 60.4 %all-to-all-start.1 = ((bf16[64,32,512]{2,1,0:T(8,128)(2,1)}), bf16[64,32,512]{2,1,0:T(8,128)(2,1)}, u32[]{:S(2)}, u32[]{:S(2)}) async-start(bf16[64,32,512]{2,1,0:T(8,128)(2,1)} %bitcast.60), calls=%async_computation.1 | async-start | bytes 4194304 | tf_op jit(solution)/shard_map/all_to_all | solution.py:50
  61.8 1.9 copy-start.11
  61.8 123.8 %all-reduce.2.cloned.1.call-start = ((), (), s32[]{:S(2)}) async-start(), calls=%async_computation.4 | async-start | bytes 1048576 | tf_op jit(solution)/shard_map/psum | solution.py:73
  66.8 46.1 %copy-start.10 = (bf16[512,512]{1,0:T(8,128)(2,1)S(1)}, bf16[512,512]{1,0:T(8,128)(2,1)}, u32[]{:S(2)}) copy-start(bf16[512,512]{1,0:T(8,128)(2,1)} %param.23) | copy-start | bytes 1572868
  66.8 46.1 %copy-start.14 = (f32[512]{0:T(512)S(1)}, f32[512]{0:T(512)}, u32[]{:S(2)}) copy-start(f32[512]{0:T(512)} %param.25) | copy-start | bytes 6148
  120.8 64.7 %copy-start.12 = (f32[1024]{0:T(1024)S(1)}, f32[1024]{0:T(1024)}, u32[]{:S(2)}) copy-start(f32[1024]{0:T(1024)} %param.27) | copy-start | bytes 12292
  120.8 64.7 %copy-start.13 = (f32[3,256]{1,0:T(4,128)S(1)}, f32[3,256]{1,0:T(4,128)}, u32[]{:S(2)}) copy-start(f32[3,256]{1,0:T(4,128)} %param.30) | copy-start | bytes 9220
  188.9 20.1 %copy-start.1 = (bf16[256,256]{1,0:T(8,128)(2,1)}, bf16[256,256]{1,0:T(8,128)(2,1)S(1)}, u32[]{:S(2)}) copy-start(bf16[256,256]{1,0:T(8,128)(2,1)S(1)} %fusion.14) | copy-start | bytes 393220
  196.4 12.1 %copy-start.6 = (s32[256,10]{0,1:T(8,128)S(1)}, s32[256,10]{0,1:T(8,128)}, u32[]{:S(2)}) copy-start(s32[256,10]{0,1:T(8,128)} %param.33) | copy-start | bytes 30724
  196.4 12.5 %copy-start.9 = (s32[256]{0:T(256)S(1)}, s32[256]{0:T(256)}, u32[]{:S(2)}) copy-start(s32[256]{0:T(256)} %param.34) | copy-start | bytes 3076
  197.7 39.3 %all-to-all-start.2 = ((bf16[64,32,256]{2,1,0:T(8,128)(2,1)}), bf16[64,32,256]{2,1,0:T(8,128)(2,1)S(1)}, u32[]{:S(2)}, u32[]{:S(2)}) async-start(bf16[64,32,256]{2,1,0:T(8,128)(2,1)} %broadcast_select_fusion), calls=%async_computation.2 | async-start | bytes 2097152 | tf_op jit(solution)/shard_map/all_to_all | solution.py:92
  208.3 64.8 %reduce-scatter.2.cloned.1.call-start = ((), (), s32[]{:S(2)}) async-start(), calls=%async_computation.5 | async-start | bytes 655360 | tf_op jit(solution)/shard_map/reduce_scatter | solution.py:97
  245.2 6.4 %copy-start.3 = (bf16[256,1024]{1,0:T(8,128)(2,1)S(1)}, bf16[256,1024]{1,0:T(8,128)(2,1)}, u32[]{:S(2)}) copy-start(bf16[256,1024]{1,0:T(8,128)(2,1)} %param.35) | copy-start | bytes 1572868
  248.8 3.1 %copy-start.4 = (bf16[256,1024]{1,0:T(8,128)(2,1)S(1)}, bf16[256,1024]{1,0:T(8,128)(2,1)}, u32[]{:S(2)}) copy-start(bf16[256,1024]{1,0:T(8,128)(2,1)} %param.36) | copy-start | bytes 1572868
  251.6 21.5 %copy-start.8 = (f32[1024]{0:T(1024)S(1)}, f32[1024]{0:T(1024)}, u32[]{:S(2)}) copy-start(f32[1024]{0:T(1024)} %param.37) | copy-start | bytes 12292
Sparse Core Ops, SparseCore 0:
  141.1 44.4 all-reduce.1
  253.2 19.7 reduce-scatter.1
where the time goes:
time: 282 us; the launch traced here: 281 us
  waiting for transfers between devices  115 us (41%)
  other arithmetic  60.5 us (21%)
  local copies, waits for them, and re-layouts  44.4 us (16%)
  starting transfers between devices  32.4 us (11%)
  matrix products  14.6 us (5%)
  between operations  14.5 us (5%)
    all_to_all x1, waiting for transfers between devices, per_device(): lax.all_to_all(feat_buffer, 'nodes', split_axis=0, concat_axis=0, tiled=T...  37.1 us
    psum x1, waiting for transfers between devices, per_device(): lax.psum(partial_total.astype(jnp.bfloat16), 'mp').astype(jnp.float32)  29.8 us
    all_to_all x1, waiting for transfers between devices, per_device(): lax.all_to_all(outgoing, 'nodes', split_axis=0, concat_axis=0, tiled=True)  26.8 us
    reduce_scatter x1, waiting for transfers between devices, per_device(): lax.psum_scatter((jnp.dot(neigh_mean, w_neigh, preferred_element_type=jnp...  20 us
    scatter-add x1, other arithmetic, per_device(): jax.ops.segment_sum(partial_msg, segment_ids, num_segments=mem_rows + 1)  19.2 us
    another operation x3, other arithmetic  18.2 us
    scatter-add x1, other arithmetic, per_device(): jax.ops.segment_sum(valid.astype(jnp.float32), segment_ids, num_segments=...  14.7 us
    all_to_all x1, starting transfers between devices, per_device(): lax.all_to_all(id_buffer, 'nodes', split_axis=0, concat_axis=0, tiled=True)  12.1 us
  transfers between devices with their start and end apart: 5, of which 5 were waited for; matrix products, arithmetic and copies ran while one was open for 13% of the time, Pallas kernels for 0%

commit v1 on v0

--- a/solution.py
+++ b/solution.py
@@ -70,7 +70,9 @@
         :mem_rows
     ]
     divisor = jnp.maximum(counts, 1.0)[:, None]
-    msg_total = lax.psum(partial_total.astype(jnp.bfloat16), "mp").astype(jnp.float32)
+    msg_total = jnp.sum(lax.all_gather(partial_total.astype(jnp.bfloat16), "mp"), axis=0).astype(
+        jnp.float32
+    )
     aggregate = (msg_total / divisor + b_out).astype(jnp.bfloat16)
     gates_in = (
         jnp.einsum("nd,gdc->gnc", aggregate, w_input, preferred_element_type=jnp.float32)

time: 282 us -> 269 us (0.954)
  waiting for transfers between devices: 115 us -> 101 us
    psum x1 -> x0, waiting for transfers between devices: 29.8 us -> none  [per_device(): lax.psum(partial_total.astype(jnp.bfloat16), 'mp').astype(jnp.float32)]
    all_gather x0 -> x1, waiting for transfers between devices: none -> 14.1 us  [per_device(): lax.all_gather(partial_total.astype(jnp.bfloat16), 'mp')]
    reduce_sum x0 -> x1, other arithmetic: none -> 2.93 us  [per_device(): jnp.sum(lax.all_gather(partial_total.astype(jnp.bfloat16), 'mp'), axis=0)]
where the time goes in v1:
time: 269 us; the launch traced here: 268 us
  waiting for transfers between devices  101 us (38%)
  other arithmetic  62.6 us (23%)
  local copies, waits for them, and re-layouts  44.4 us (17%)
  starting transfers between devices  32.4 us (12%)
  between operations  14.5 us (5%)
  matrix products  13.4 us (5%)
    all_to_all x1, waiting for transfers between devices, per_device(): lax.all_to_all(feat_buffer, 'nodes', split_axis=0, concat_axis=0, tiled=T...  39 us
    all_to_all x1, waiting for transfers between devices, per_device(): lax.all_to_all(outgoing, 'nodes', split_axis=0, concat_axis=0, tiled=True)  26.8 us
    reduce_scatter x1, waiting for transfers between devices, per_device(): lax.psum_scatter((jnp.dot(neigh_mean, w_neigh, preferred_element_type=jnp...  19.5 us
    scatter-add x1, other arithmetic, per_device(): jax.ops.segment_sum(partial_msg, segment_ids, num_segments=mem_rows + 1)  19.3 us
    another operation x3, other arithmetic  18.2 us
    scatter-add x1, other arithmetic, per_device(): jax.ops.segment_sum(valid.astype(jnp.float32), segment_ids, num_segments=...  14.7 us
    all_gather x1, waiting for transfers between devices, per_device(): lax.all_gather(partial_total.astype(jnp.bfloat16), 'mp')  14.1 us
    all_to_all x1, starting transfers between devices, per_device(): lax.all_to_all(id_buffer, 'nodes', split_axis=0, concat_axis=0, tiled=True)  12.1 us
  transfers between devices with their start and end apart: 5, of which 5 were waited for; matrix products, arithmetic and copies ran while one was open for 13% of the time, Pallas kernels for 0%

profile of v1, /device:TPU:8, one launch (start us, length us, event | category | flops | bytes accessed | tf_op | source)
XLA Modules:
  0.0 268.0 jit_solution(11205271239898431010)
XLA Ops:
  8.0 18.0 %reduce-window.6 = s32[64,8,128]{2,1,0:T(8,128)S(1)} reduce-window(s32[64,8,128]{2,1,0:T(8,128)S(1)} %fusion.31, s32[]{:T(128)} %constant.49.clone.1), window={size=1x1x128 pad=0_0x0_0x127_0}, to_apply=%region_0.0 | reduce-window | flops 8323072 | bytes 524292 | tf_op jit(solution)/shard_map/reduce-window
  26.7 4.5 %scatter_custom_fusion = s32[2048]{0:T(1024)S(1)} fusion(s32[1024]{0:T(1024)S(1)} %bitcast.73, s32[1024]{0:T(1024)} %param.21, s32[]{:T(128)} %constant.47.clone.1), kind=kCustom, calls=%fused_computation.79 | custom fusion | bytes 8704 | tf_op jit(solution)/shard_map/scatter | solution.py:44
  31.9 12.1 %all-to-all-start = ((s32[64,1,32]{2,1,0:T(1,128)}), s32[64,1,32]{2,1,0:T(1,128)S(1)}, u32[]{:S(2)}, u32[]{:S(2)}) async-start(s32[64,1,32]{2,1,0:T(1,128)} %bitcast.6), calls=%async_computation | async-start | bytes 65536 | tf_op jit(solution)/shard_map/all_to_all | solution.py:51
  44.0 7.2 %scatter_custom_fusion.2 = bf16[2048,512]{1,0:T(8,128)(2,1)} fusion(s32[1024]{0:T(1024)S(1)} %bitcast.74, bf16[1024,512]{1,0:T(8,128)(2,1)} %param.19, bf16[]{:T(256)} %constant.59.clone.1), kind=kCustom, calls=%fused_computation.18 | custom fusion | bytes 2097664 | tf_op jit(solution)/shard_map/scatter | solution.py:47
  51.2 1.4 all-to-all-done
  52.5 9.3 %all-to-all-start.1 = ((bf16[64,32,512]{2,1,0:T(8,128)(2,1)}), bf16[64,32,512]{2,1,0:T(8,128)(2,1)}, u32[]{:S(2)}, u32[]{:S(2)}) async-start(bf16[64,32,512]{2,1,0:T(8,128)(2,1)} %bitcast.61), calls=%async_computation.1 | async-start | bytes 4194304 | tf_op jit(solution)/shard_map/all_to_all | solution.py:50
  62.0 1.5 fusion.45
  65.0 9.0 %gather_fusion = f32[2048,512]{1,0:T(8,128)} fusion(f32[256,512]{1,0:T(8,128)S(1)} %fusion.45, s32[2048]{0:T(1024)S(1)} %broadcast_clamp_fusion.1), kind=kCustom, calls=%fused_computation | custom fusion | bytes 8396800 | tf_op jit(solution)/shard_map/jit(_take)/gather | solution.py:61
  73.9 39.0 %all-to-all-done.1 = bf16[64,32,512]{2,1,0:T(8,128)(2,1)} async-done(((bf16[64,32,512]{2,1,0:T(8,128)(2,1)}), bf16[64,32,512]{2,1,0:T(8,128)(2,1)}, u32[]{:S(2)}, u32[]{:S(2)}) %all-to-all-start.1) | async-done | bytes 2097184 | tf_op jit(solution)/shard_map/all_to_all | solution.py:50
  112.9 7.7 %fusion.5 = f32[2048,1024]{1,0:T(8,128)} fusion(bf16[512,1024]{1,0:T(8,128)(2,1)S(1)} %copy-done.11, f32[2048,512]{1,0:T(8,128)} %gather_fusion, bf16[2048,512]{1,0:T(8,128)(2,1)} %bitcast.9, bf16[512,512]{1,0:T(8,128)(2,1)} %param.23, f32[512]{0:T(512)S(1)} %copy-done.15, pred[2048]{0:T(1024)(128)(4,1)S(1)} %get-tuple-element.3), kind=kOutput, calls=%fused_computation.21 | convolution fusion | flops 3226468352 | bytes 16257024 | tf_op jit(solution)/shard_map/dot_general | solution.py:65
  120.6 19.3 %scatter_custom_fusion.3 = f32[257,1024]{1,0:T(8,128)S(1)} fusion(s32[2048]{0:T(1024)S(1)} %bitcast.71, f32[2048,1024]{1,0:T(8,128)} %fusion.5, f32[]{:T(128)} %constant.46.clone.1), kind=kCustom, calls=%fused_computation.22 | custom fusion | flops 2097152 | bytes 1053184 | tf_op jit(solution)/shard_map/scatter-add | solution.py:66
  141.8 14.7 %scatter_custom_fusion.1 = f32[257]{0:T(512)S(1)} fusion(s32[2048]{0:T(1024)S(1)} %bitcast.72, f32[2048]{0:T(1024)S(1)} %get-tuple-element.2, f32[]{:T(128)} %constant.46.clone.1), kind=kCustom, calls=%fused_computation.83 | custom fusion | flops 2048 | bytes 1032 | tf_op jit(solution)/shard_map/scatter-add | solution.py:69
  156.5 14.1 %all-gather.3.cloned.1.call-done = bf16[1024,1024]{1,0:T(8,128)(2,1)} async-done(((bf16[256,1024]{1,0:T(8,128)(2,1)}), bf16[1024,1024]{1,0:T(8,128)(2,1)}) %all-gather.3.cloned.1.call-update) | async-done | bytes 2097168 | tf_op jit(solution)/shard_map/all_gather | solution.py:73
  170.5 2.9 %reduce_sum.34 = bf16[256,1024]{1,0:T(8,128)(2,1)} reduce(bf16[4,256,1024]{2,1,0:T(8,128)(2,1)} %bitcast.63, bf16[]{:T(256)} %constant.59.clone.1), dimensions={0}, to_apply=%region_7.8 | reduce | flops 786432 | bytes 2621442 | tf_op jit(solution)/shard_map/reduce_sum | solution.py:73
  173.5 2.2 fusion.2
  175.9 7.5 %gather_fusion.1 = bf16[2048,256]{1,0:T(8,128)(2,1)S(1)} fusion(bf16[256,256]{1,0:T(8,128)(2,1)S(1)} %fusion.14, s32[2048]{0:T(1024)S(1)} %broadcast_clamp_fusion), kind=kCustom, calls=%fused_computation.1 | custom fusion | bytes 2105344 | tf_op jit(solution)/shard_map/jit(_take)/gather | solution.py:93
  183.4 1.3 broadcast_select_fusion
  184.7 10.6 %all-to-all-start.2 = ((bf16[64,32,256]{2,1,0:T(8,128)(2,1)}), bf16[64,32,256]{2,1,0:T(8,128)(2,1)S(1)}, u32[]{:S(2)}, u32[]{:S(2)}) async-start(bf16[64,32,256]{2,1,0:T(8,128)(2,1)} %broadcast_select_fusion), calls=%async_computation.2 | async-start | bytes 2097152 | tf_op jit(solution)/shard_map/all_to_all | solution.py:94
  197.2 26.8 %all-to-all-done.2 = bf16[64,32,256]{2,1,0:T(8,128)(2,1)S(1)} async-done(((bf16[64,32,256]{2,1,0:T(8,128)(2,1)}), bf16[64,32,256]{2,1,0:T(8,128)(2,1)S(1)}, u32[]{:S(2)}, u32[]{:S(2)}) %all-to-all-start.2) | async-done | bytes 1048608 | tf_op jit(solution)/shard_map/all_to_all | solution.py:94
  224.0 8.1 %gather_fusion.2 = bf16[2560,256]{1,0:T(8,128)(2,1)} fusion(bf16[2048,256]{1,0:T(8,128)(2,1)S(1)} %bitcast.60, s32[3072]{0:T(1024)S(1)} %pad_clamp_fusion), kind=kCustom, calls=%fused_computation.2 | custom fusion | bytes 2631680 | tf_op jit(solution)/shard_map/jit(_take)/gather | solution.py:96
  232.2 3.6 %reshape.152 = bf16[256,10,256]{2,1,0:T(8,128)(2,1)} reshape(bf16[2560,256]{1,0:T(8,128)(2,1)} %gather_fusion.2) | data formatting | bytes 2621440 | tf_op jit(solution)/shard_map/jit(_take)/gather | solution.py:96
  235.8 2.7 %convert_reduce_fusion = f32[256,256]{1,0:T(8,128)S(1)} fusion(bf16[256,10,256]{2,1,0:T(8,128)(2,1)} %reshape.152, pred[256,10]{1,0:T(8,128)(4,1)S(1)} %copy.47), kind=kLoop, calls=%fused_computation.8 | loop fusion | flops 1900544 | bytes 1575424 | tf_op jit(solution)/shard_map/reduce_sum | solution.py:97
  240.1 19.5 %reduce-scatter.2.cloned.1.call-done = bf16[64,1024]{1,0:T(8,128)(2,1)} async-done(((bf16[256,1024]{1,0:T(8,128)(2,1)}), bf16[64,1024]{1,0:T(8,128)(2,1)}) %reduce-scatter.2.cloned.1.call-update) | async-done | bytes 131088 | tf_op jit(solution)/shard_map/reduce_scatter | solution.py:99
  259.5 1.6 maximum_convert_fusion.1
  (76 shorter events, 9.1 us)
Async XLA Ops:
  7.2 134.0 %copy-start = (bf16[3,1024,256]{2,1,0:T(8,128)(2,1)S(1)}, bf16[3,1024,256]{2,1,0:T(8,128)(2,1)}, u32[]{:S(2)}) copy-start(bf16[3,1024,256]{2,1,0:T(8,128)(2,1)} %param.29) | copy-start | bytes 4718596
  7.2 19.4 %copy-start.8 = (s32[1024,1]{0,1:T(1,128)S(1)}, s32[1024,1]{0,1:T(1,128)}, u32[]{:S(2)}) copy-start(s32[1024,1]{0,1:T(1,128)} %param.20) | copy-start | bytes 12292
  31.9 20.7 %all-to-all-start = ((s32[64,1,32]{2,1,0:T(1,128)}), s32[64,1,32]{2,1,0:T(1,128)S(1)}, u32[]{:S(2)}, u32[]{:S(2)}) async-start(s32[64,1,32]{2,1,0:T(1,128)} %bitcast.6), calls=%async_computation | async-start | bytes 65536 | tf_op jit(solution)/shard_map/all_to_all | solution.py:51
  52.5 9.5 %copy-start.2 = (bf16[1024,512]{1,0:T(8,128)(2,1)S(1)}, bf16[1024,512]{1,0:T(8,128)(2,1)}, u32[]{:S(2)}) copy-start(bf16[1024,512]{1,0:T(8,128)(2,1)} %param.24) | copy-start | bytes 3145732
  52.5 60.4 %all-to-all-start.1 = ((bf16[64,32,512]{2,1,0:T(8,128)(2,1)}), bf16[64,32,512]{2,1,0:T(8,128)(2,1)}, u32[]{:S(2)}, u32[]{:S(2)}) async-start(bf16[64,32,512]{2,1,0:T(8,128)(2,1)} %bitcast.61), calls=%async_computation.1 | async-start | bytes 4194304 | tf_op jit(solution)/shard_map/all_to_all | solution.py:50
  61.8 108.8 %all-gather.3.cloned.1.call-start = ((), (), s32[]{:S(2)}) async-start(), calls=%async_computation.5 | async-start | bytes 2621440 | tf_op jit(solution)/shard_map/all_gather | solution.py:73
  64.9 48.0 %copy-start.11 = (bf16[512,1024]{1,0:T(8,128)(2,1)S(1)}, bf16[512,1024]{1,0:T(8,128)(2,1)}, u32[]{:S(2)}) copy-start(bf16[512,1024]{1,0:T(8,128)(2,1)} %param.26) | copy-start | bytes 3145732
  65.0 48.0 %copy-start.15 = (f32[512]{0:T(512)S(1)}, f32[512]{0:T(512)}, u32[]{:S(2)}) copy-start(f32[512]{0:T(512)} %param.25) | copy-start | bytes 6148
  120.6 20.2 %copy-start.6 = (s32[64,32]{0,1:T(8,128)S(1)}, s32[64,32]{0,1:T(8,128)}, u32[]{:S(2)}) copy-start(s32[64,32]{0,1:T(8,128)} %param.32) | copy-start | bytes 24580
  120.6 20.5 %copy-start.3 = (bf16[256,1024]{1,0:T(8,128)(2,1)S(1)}, bf16[256,1024]{1,0:T(8,128)(2,1)}, u32[]{:S(2)}) copy-start(bf16[256,1024]{1,0:T(8,128)(2,1)} %param.22) | copy-start | bytes 1572868
  120.6 20.5 %copy-start.12 = (f32[3,256]{1,0:T(4,128)S(1)}, f32[3,256]{1,0:T(4,128)}, u32[]{:S(2)}) copy-start(f32[3,256]{1,0:T(4,128)} %param.31) | copy-start | bytes 9220
  141.2 32.3 %copy-start.13 = (f32[1024]{0:T(1024)S(1)}, f32[1024]{0:T(1024)}, u32[]{:S(2)}) copy-start(f32[1024]{0:T(1024)} %param.27) | copy-start | bytes 12292
  141.2 32.3 %copy-start.14 = (f32[3,256]{1,0:T(4,128)S(1)}, f32[3,256]{1,0:T(4,128)}, u32[]{:S(2)}) copy-start(f32[3,256]{1,0:T(4,128)} %param.30) | copy-start | bytes 9220
  175.9 20.1 %copy-start.1 = (bf16[256,256]{1,0:T(8,128)(2,1)}, bf16[256,256]{1,0:T(8,128)(2,1)S(1)}, u32[]{:S(2)}) copy-start(bf16[256,256]{1,0:T(8,128)(2,1)S(1)} %fusion.14) | copy-start | bytes 393220
  183.4 12.1 %copy-start.7 = (s32[256,10]{0,1:T(8,128)S(1)}, s32[256,10]{0,1:T(8,128)}, u32[]{:S(2)}) copy-start(s32[256,10]{0,1:T(8,128)} %param.33) | copy-start | bytes 30724
  183.4 12.5 %copy-start.10 = (s32[256]{0:T(256)S(1)}, s32[256]{0:T(256)}, u32[]{:S(2)}) copy-start(s32[256]{0:T(256)} %param.34) | copy-start | bytes 3076
  184.7 39.3 %all-to-all-start.2 = ((bf16[64,32,256]{2,1,0:T(8,128)(2,1)}), bf16[64,32,256]{2,1,0:T(8,128)(2,1)S(1)}, u32[]{:S(2)}, u32[]{:S(2)}) async-start(bf16[64,32,256]{2,1,0:T(8,128)(2,1)} %broadcast_select_fusion), calls=%async_computation.2 | async-start | bytes 2097152 | tf_op jit(solution)/shard_map/all_to_all | solution.py:94
  195.3 64.3 %reduce-scatter.2.cloned.1.call-start = ((), (), s32[]{:S(2)}) async-start(), calls=%async_computation.4 | async-start | bytes 655360 | tf_op jit(solution)/shard_map/reduce_scatter | solution.py:99
  232.2 6.4 %copy-start.4 = (bf16[256,1024]{1,0:T(8,128)(2,1)S(1)}, bf16[256,1024]{1,0:T(8,128)(2,1)}, u32[]{:S(2)}) copy-start(bf16[256,1024]{1,0:T(8,128)(2,1)} %param.35) | copy-start | bytes 1572868
  235.8 3.1 %copy-start.5 = (bf16[256,1024]{1,0:T(8,128)(2,1)S(1)}, bf16[256,1024]{1,0:T(8,128)(2,1)}, u32[]{:S(2)}) copy-start(bf16[256,1024]{1,0:T(8,128)(2,1)} %param.36) | copy-start | bytes 1572868
  238.6 21.0 %copy-start.9 = (f32[1024]{0:T(1024)S(1)}, f32[1024]{0:T(1024)}, u32[]{:S(2)}) copy-start(f32[1024]{0:T(1024)} %param.37) | copy-start | bytes 12292
Sparse Core Ops, SparseCore 0:
  141.0 29.5 all-gather.2
  240.2 19.3 reduce-scatter.1
